TPU v7x, 128 devices: a whole 4x4x4 slice. The times are simulated.
128 devices in a mesh: dp: 32 (over y, x, core), tensor: 4 (over z).
Axes of the slice: x: 4, y: 4, z: 4, core: 2. Of those that a mesh axis runs over, the one named last changes fastest.
Arguments:
- layer_input: bfloat16 [4096, 2560], P('dp'), may hold values from -6 to 6
- inner_out: bfloat16 [4096, 2560], P('dp', 'tensor'), may hold values from -6 to 6
- out_grad: bfloat16 [4096, 2560], P('dp'), may hold values from -0.09375 to 0.09375
- zx_grad: bfloat16 [4096, 5120], P('dp', 'tensor'), may hold values from -0.09375 to 0.09375
- bc_grad: bfloat16 [4096, 1024], P('dp', 'tensor'), may hold values from -0.09375 to 0.09375
- dt_grad: bfloat16 [4096, 40], P('dp', 'tensor'), may hold values from -0.09375 to 0.09375
- owner_deal: int32 [4, 31], P('tensor'), may hold values from 0 to 31, as said below
- head_momentum: float32 [4, 2368, 2560], P('tensor', 'dp'), may hold values from -6 to 6
- bc_momentum: float32 [2, 128, 2560], replicated, may hold values from -6 to 6
Outputs:
- head_update: bfloat16 [40, 3, 64, 2560], P('tensor')
- dt_update: bfloat16 [40, 2560], P('tensor')
- bc_update: bfloat16 [2, 128, 2560], replicated
- head_momentum_out: float32 [4, 2368, 2560], P('tensor', 'dp')
- bc_momentum_out: float32 [2, 128, 2560], replicated
Inputs may be any that keep to these rules, and one draw needn't show every extreme that they name: `owner_deal`: each owner holds at most 1 head blocks of one tensor index; the owner of the dt block (the last entry) holds exactly 1 head blocks of that index as well, so it holds exactly 74 rows.
All inputs are finite; a program needn't handle non-finite values.
Results may differ from a plain program's by a relative error of at most 0.0085.
Values may be sent and summed in bfloat16 or wider, within the bound.
No kernel may reach another device: no remote copies, remote signals or barrier semaphores. Data moves between devices by JAX's collectives and lax.ppermute only.
A program may use at most 128 MiB of HBM per device.

v0:
```python
import math
import jax
import jax.numpy as jnp
from jax import lax
from jax.sharding import PartitionSpec as P

HD = 64
STATE = 128
NS_ITERS = 5
quintic_first = 3.4445
quintic_second = -4.775
quintic_third = 2.0315
momentum_decay = 0.95
norm_epsilon = 1e-07


def orthogonalize(moment):
    highest = lax.Precision.HIGHEST
    norm_value = jnp.sqrt(jnp.sum(moment * moment, axis=(1, 2), keepdims=True))
    current = moment / (norm_value + norm_epsilon)
    for step in range(NS_ITERS):
        gram_matrix = jnp.einsum("bik,bjk->bij", current, current, precision=highest)
        polynomial = quintic_second * gram_matrix + quintic_third * jnp.einsum(
            "bij,bjk->bik", gram_matrix, gram_matrix, precision=highest
        )
        current = quintic_first * current + jnp.einsum(
            "bij,bjk->bik", polynomial, current, precision=highest
        )
    return current


def on_device(
    layer_input,
    inner_out,
    out_grad,
    zx_grad,
    bc_grad,
    dt_grad,
    owner_deal,
    head_momentum,
    bc_momentum,
):
    n_data = lax.axis_size("dp")
    tokens, width = layer_input.shape
    heads_here = dt_grad.shape[1]
    capacity = head_momentum.shape[1]
    n_blocks = 3 * heads_here
    contract = (((0,), (0,)), ((), ()))
    f32, bf16 = (jnp.float32, jnp.bfloat16)
    owners = owner_deal[0]
    head_owner = owners[:n_blocks]
    dt_owner = owners[n_blocks]
    slots = jnp.arange(n_data, dtype=jnp.int32)
    bc_cols = jnp.sum(lax.all_gather(bc_grad, "tensor", axis=0).astype(f32), axis=0)
    bc_part = lax.dot_general(
        bc_cols,
        layer_input.astype(f32),
        contract,
        precision=lax.Precision.HIGHEST,
        preferred_element_type=f32,
    )
    bc_summed = lax.psum(bc_part, "dp")
    zx = zx_grad.reshape(tokens, heads_here, 2, HD)
    io = inner_out.reshape(tokens, heads_here, 1, HD)
    upper = jnp.concatenate([zx, jnp.zeros_like(io)], axis=2).reshape(tokens, n_blocks, HD)
    lower = jnp.concatenate([jnp.zeros_like(zx), io], axis=2).reshape(tokens, n_blocks, HD)
    grad_blocks = jnp.concatenate([upper, lower], axis=0)
    pick = (head_owner[None, :] == slots[:, None]).astype(bf16)
    owner_cols = jnp.einsum("tbr,ob->tor", grad_blocks, pick, preferred_element_type=f32).astype(
        bf16
    )
    dt_cols = jnp.concatenate([dt_grad, jnp.zeros_like(dt_grad)], axis=0)
    is_dt = (slots == dt_owner).astype(bf16)
    dt_owner_cols = dt_cols[:, None, :] * is_dt[None, :, None]
    chunk = -(-capacity // 16) * 16
    pad_cols = jnp.zeros((2 * tokens, n_data, chunk - capacity), bf16)
    send_cols = jnp.concatenate([owner_cols, dt_owner_cols, pad_cols], axis=2).reshape(
        2 * tokens, n_data * chunk
    )
    factors = jnp.concatenate([layer_input, out_grad], axis=0)
    send = lax.dot_general(send_cols, factors, contract, preferred_element_type=f32).astype(bf16)
    owned_sum = lax.psum_scatter(send, "dp", scatter_dimension=0, tiled=True)[:capacity].astype(f32)
    moment = momentum_decay * head_momentum[0] + owned_sum
    head_direction = orthogonalize(moment[None, :HD])[0]
    dt_direction = orthogonalize(moment[None, HD:])[0]
    head_gathered = lax.all_gather(
        (head_direction * math.sqrt(width)).astype(bf16), "dp", axis=0, tiled=False
    )
    tail = jnp.concatenate([dt_direction, jnp.zeros((chunk - capacity, width), f32)], axis=0)
    tail_gathered = lax.all_gather(
        (tail * math.sqrt(width)).astype(bf16), "dp", axis=0, tiled=False
    )
    head_update = jnp.take(head_gathered, head_owner, axis=0, mode="clip").reshape(
        heads_here, 3, HD, width
    )
    dt_update = lax.dynamic_slice(tail_gathered, (dt_owner, 0, 0), (1, heads_here, width))[0]
    bc_moment = momentum_decay * bc_momentum + bc_summed.reshape(2, STATE, width)
    bc_update = (orthogonalize(bc_moment) * math.sqrt(width)).astype(bf16)
    return (head_update, dt_update, bc_update, moment[None], bc_moment)


def solution(mesh):
    in_specs = (
        P("dp", None),
        P("dp", "tensor"),
        P("dp", None),
        P("dp", "tensor"),
        P("dp", "tensor"),
        P("dp", "tensor"),
        P("tensor", None),
        P("tensor", "dp", None),
        P(),
    )
    out_specs = (
        P("tensor", None, None, None),
        P("tensor", None),
        P(),
        P("tensor", "dp", None),
        P(),
    )
    return jax.shard_map(
        on_device, mesh=mesh, in_specs=in_specs, out_specs=out_specs, check_vma=False
    )
```

profile of v0, /device:TPU:1, one launch (start us, length us, event | category | flops | bytes accessed | tf_op | source)
XLA Modules:
  0.0 366.2 jit_solution(17709010283561353093)
XLA Ops:
  7.2 1.2 slice.18
  8.4 0.7 slice_bitcast_fusion
  9.1 0.6 compare_convert_fusion
  9.8 1.1 copy.20
  10.8 0.7 concatenate.24
  11.6 0.3 copy.23
  12.0 1.2 copy.19
  13.2 0.3 copy.22
  13.7 0.4 fusion.4
  14.4 0.7 copy.24
  15.4 6.7 %convolution_convert_fusion = bf16[2560,2560]{1,0:T(8,128)(2,1)} fusion(bf16[256,2560]{0,1:T(8,128)(2,1)S(1)} %bitcast.114, bf16[128,2560]{1,0:T(8,128)(2,1)S(1)} %copy-done.4, bf16[128,2560]{1,0:T(8,128)(2,1)S(1)} %copy-done), kind=kOutput, calls=%fused_computation.1 | convolution fusion | flops 3364618240 | bytes 15728640 | tf_op jit(solution)/shard_map/dot_general | solution.py:81
  22.2 0.8 copy-done.5
  23.0 12.3 %all-gather.2 = bf16[512,256]{1,0:T(8,128)(2,1)S(1)} all-gather(bf16[128,256]{1,0:T(8,128)(2,1)S(1)} %copy-done.5), channel_id=4, replica_groups=mesh['dp'=32,'tensor'=4] {'tensor'}, dimensions={0}, use_global_device_ids=true | all-gather | bytes 327680 | tf_op jit(solution)/shard_map/all_gather | solution.py:54
  35.3 2.7 fusion.42
  38.1 91.4 %reduce-scatter.2.cloned.1.call-done = bf16[80,2560]{1,0:T(8,128)(2,1)} async-done(((bf16[2560,2560]{1,0:T(8,128)(2,1)}), bf16[80,2560]{1,0:T(8,128)(2,1)}) %reduce-scatter.2.cloned.1.call-update) | async-done | bytes 409616 | tf_op jit(solution)/shard_map/reduce_scatter | solution.py:82
  129.5 1.1 bitcast_add_fusion
  130.7 0.6 multiply_reduce_fusion.2
  132.0 0.3 fusion.28
  135.8 0.7 multiply_convert_fusion
  136.5 0.5 all-gather.6.cloned.1.call-start
  137.0 0.8 multiply_reduce_fusion.1
  138.5 0.7 fusion.27
  139.3 0.7 convolution_add_fusion.9
  140.1 0.7 fusion.34
  140.9 0.7 convolution_add_fusion.8
  141.6 0.7 fusion.35
  142.4 0.7 convolution_add_fusion.7
  143.1 0.7 fusion.36
  144.0 0.7 convolution_add_fusion.6
  144.7 0.7 fusion.37
  145.5 1.4 fusion.3
  148.9 93.6 %all-reduce.6.cloned.1.call-done = f32[2,128,2560]{2,1,0:T(8,128)} async-done(((f32[2,128,2560]{2,1,0:T(8,128)}), f32[2,128,2560]{2,1,0:T(8,128)}) %all-reduce.6.cloned.1.call-update) | async-done | bytes 2621456 | tf_op jit(solution)/shard_map/psum | solution.py:62
  242.5 2.3 multiply_reduce_fusion
  244.8 2.8 fusion.26
  247.9 2.8 convolution_add_fusion.4
  250.7 2.5 fusion.43
  253.5 2.6 convolution_add_fusion.3
  256.2 2.5 fusion.44
  259.0 2.6 convolution_add_fusion.2
  261.6 2.7 fusion.45
  264.6 2.6 convolution_add_fusion.1
  267.3 2.5 fusion.46
  270.1 3.7 %fusion.1 = bf16[2,128,2560]{2,1,0:T(8,128)(2,1)} fusion(f32[2,128,128]{2,1,0:T(8,128)S(1)} %fusion.8, f32[2,128,2560]{2,1,0:T(8,128)S(1)} %convolution_add_fusion.1), kind=kOutput, calls=%fused_computation.8 | convolution fusion | flops 1009254400 | bytes 4063232 | tf_op jit(solution)/shard_map/bij,bjk->bik/dot_general | solution.py:26
  273.8 1.6 copy.25
  275.4 14.4 %all-gather.8.cloned.1.call-done = bf16[512,2560]{1,0:T(8,128)(2,1)} async-done(((bf16[16,2560]{1,0:T(8,128)(2,1)}), bf16[512,2560]{1,0:T(8,128)(2,1)}) %all-gather.8.cloned.1.call-update) | async-done | bytes 2621456 | tf_op jit(solution)/shard_map/all_gather | solution.py:90
  289.8 1.5 dynamic-slice_bitcast_fusion
  291.4 58.2 %all-gather.6.cloned.1.call-done = bf16[2048,2560]{1,0:T(8,128)(2,1)} async-done(((bf16[64,2560]{1,0:T(8,128)(2,1)}), bf16[2048,2560]{1,0:T(8,128)(2,1)}) %all-gather.6.cloned.1.call-update) | async-done | bytes 10485776 | tf_op jit(solution)/shard_map/all_gather | solution.py:86
  349.5 9.9 %gather_fusion = bf16[30,64,2560]{2,1,0:T(8,128)(2,1)} fusion(bf16[32,64,2560]{2,1,0:T(8,128)(2,1)} %bitcast.112, s32[1024]{0:T(1024)S(1)} %pad_clamp_fusion), kind=kCustom, calls=%fused_computation | custom fusion | bytes 19660920 | tf_op jit(solution)/shard_map/jit(_take)/gather | solution.py:93
  (51 shorter events, 6.7 us)
Async XLA Ops:
  7.2 122.4 %reduce-scatter.2.cloned.1.call-start = ((), (), s32[]{:S(2)}) async-start(), calls=%async_computation.1 | async-start | bytes 13516800 | tf_op jit(solution)/shard_map/reduce_scatter | solution.py:82
  14.1 1.1 copy-start
  14.1 1.3 copy-start.4
  22.1 0.8 copy-start.5
  22.2 220.3 %all-reduce.6.cloned.1.call-start = ((), (), s32[]{:S(2)}) async-start(), calls=%async_computation.2 | async-start | bytes 5242880 | tf_op jit(solution)/shard_map/psum | solution.py:62
  35.3 94.2 %copy-start.3 = (f32[1,74,2560]{2,0,1:T(1,128)S(1)}, f32[1,74,2560]{2,0,1:T(1,128)}, u32[]{:S(2)}) copy-start(f32[1,74,2560]{2,0,1:T(1,128)} %param.16) | copy-start | bytes 2273284
  38.1 251.8 %all-gather.8.cloned.1.call-start = ((), (), s32[]{:S(2)}) async-start(), calls=%async_computation.4 | async-start | bytes 2703360 | tf_op jit(solution)/shard_map/all_gather | solution.py:90
  136.5 213.0 %all-gather.6.cloned.1.call-start = ((), (), s32[]{:S(2)}) async-start(), calls=%async_computation.3 | async-start | bytes 10813440 | tf_op jit(solution)/shard_map/all_gather | solution.py:86
  143.1 99.4 %copy-start.1 = (f32[2,128,2560]{2,1,0:T(8,128)S(1)}, f32[2,128,2560]{2,1,0:T(8,128)}, u32[]{:S(2)}) copy-start(f32[2,128,2560]{2,1,0:T(8,128)} %param.17) | copy-start | bytes 7864324
  244.8 3.1 copy-start.2
Sparse Core Ops, SparseCore 0:
  22.3 107.2 reduce-scatter.1
  133.4 109.0 all-reduce.5
  245.3 44.4 all-gather.7
  292.5 56.9 all-gather.5
where the time goes:
time: 372 us; the launch traced here: 366 us
  waiting for transfers between devices  258 us (69%)
  matrix products  50.8 us (14%)
  local copies, waits for them, and re-layouts  20.6 us (6%)
  between operations  17.7 us (5%)
  blocking collectives  12.3 us (3%)
  other arithmetic  6.46 us (2%)
    psum x1, waiting for transfers between devices, on_device(): bc_summed = lax.psum(bc_part, 'dp')  93.6 us
    reduce_scatter x1, waiting for transfers between devices, on_device(): lax.psum_scatter(send, 'dp', scatter_dimension=0, tiled=True)[:capacity]  91.4 us
    all_gather x1, waiting for transfers between devices, on_device(): lax.all_gather((head_direction * math.sqrt(width)).astype(bf16), 'dp', ax...  58.2 us
    dot_general x15, matrix products, orthogonalize(): jnp.einsum('bij,bjk->bik', polynomial, current, precision=highest)  20.1 us
    dot_general x15, matrix products, orthogonalize(): jnp.einsum('bik,bjk->bij', current, current, precision=highest)  17.7 us
    all_gather x1, waiting for transfers between devices, on_device(): lax.all_gather((tail * math.sqrt(width)).astype(bf16), 'dp', axis=0, tile...  14.4 us
    all_gather x1, blocking collectives, on_device(): lax.all_gather(bc_grad, 'tensor', axis=0).astype(f32)  12.3 us
    gather x1, local copies, waits for them, and re-layouts, on_device(): jnp.take(head_gathered, head_owner, axis=0, mode='clip')  9.86 us
  transfers between devices with their start and end apart: 4, of which 4 were waited for; matrix products, arithmetic and copies ran while one was open for 14% of the time, Pallas kernels for 0%

commit v1 on v0

--- a/solution.py
+++ b/solution.py
@@ -59,7 +59,10 @@
         precision=lax.Precision.HIGHEST,
         preferred_element_type=f32,
     )
-    bc_summed = lax.psum(bc_part, "dp")
+    size, bc_summed = (lax.axis_size("dp"), bc_part)
+    for far in [1 << k for k in range(size.bit_length() - 1)]:
+        swap = [(i, i ^ far) for i in range(size)]
+        bc_summed = bc_summed + lax.ppermute(bc_summed, "dp", swap)
     zx = zx_grad.reshape(tokens, heads_here, 2, HD)
     io = inner_out.reshape(tokens, heads_here, 1, HD)
     upper = jnp.concatenate([zx, jnp.zeros_like(io)], axis=2).reshape(tokens, n_blocks, HD)

time: 372 us -> 490 us (1.32)
  waiting for transfers between devices: 258 us -> 364 us
  starting transfers between devices: 0.63 us -> 12.6 us
    ppermute x0 -> x5, waiting for transfers between devices: none -> 257 us  [on_device(): bc_summed = bc_summed + lax.ppermute(bc_summed, 'dp', swap)]
    psum x1 -> x0, waiting for transfers between devices: 93.6 us -> none  [on_device(): bc_summed = lax.psum(bc_part, 'dp')]
    all_gather x1, waiting for transfers between devices: 58.2 us -> 0.01 us  [on_device(): lax.all_gather((head_direction * math.sqrt(width)).astype(bf16), 'dp', ax...]
    reduce_scatter x1, waiting for transfers between devices: 91.4 us -> 107 us  [on_device(): lax.psum_scatter(send, 'dp', scatter_dimension=0, tiled=True)[:capacity]]
    all_gather x1, waiting for transfers between devices: 14.4 us -> 0.01 us  [on_device(): lax.all_gather((tail * math.sqrt(width)).astype(bf16), 'dp', axis=0, tile...]
    ppermute x0 -> x5, starting transfers between devices: none -> 11.9 us  [on_device(): bc_summed = bc_summed + lax.ppermute(bc_summed, 'dp', swap)]
  transfers between devices with their start and end apart: 4 -> 8, of which waited for: 4 -> 6; matrix products, arithmetic and copies ran while one was open for 14% -> 10% of each run, Pallas kernels for 0% -> 0%
where the time goes in v1:
time: 490 us; the launch traced here: 483 us
  waiting for transfers between devices  364 us (74%)
  matrix products  50.1 us (10%)
  local copies, waits for them, and re-layouts  19.9 us (4%)
  between operations  17.8 us (4%)
  starting transfers between devices  12.6 us (3%)
  blocking collectives  10.7 us (2%)
  other arithmetic  8.12 us (2%)
    ppermute x5, waiting for transfers between devices, on_device(): bc_summed = bc_summed + lax.ppermute(bc_summed, 'dp', swap)  257 us
    reduce_scatter x1, waiting for transfers between devices, on_device(): lax.psum_scatter(send, 'dp', scatter_dimension=0, tiled=True)[:capacity]  107 us
    dot_general x15, matrix products, orthogonalize(): jnp.einsum('bij,bjk->bik', polynomial, current, precision=highest)  20.2 us
    dot_general x15, matrix products, orthogonalize(): jnp.einsum('bik,bjk->bij', current, current, precision=highest)  18.5 us
    ppermute x5, starting transfers between devices, on_device(): bc_summed = bc_summed + lax.ppermute(bc_summed, 'dp', swap)  11.9 us
    all_gather x1, blocking collectives, on_device(): lax.all_gather(bc_grad, 'tensor', axis=0).astype(f32)  10.7 us
    gather x1, local copies, waits for them, and re-layouts, on_device(): jnp.take(head_gathered, head_owner, axis=0, mode='clip')  9.86 us
  transfers between devices with their start and end apart: 8, of which 6 were waited for; matrix products, arithmetic and copies ran while one was open for 10% of the time, Pallas kernels for 0%

profile of v1, /device:TPU:1, one launch (start us, length us, event | category | flops | bytes accessed | tf_op | source)
XLA Modules:
  0.0 482.8 jit_solution(11957001899699953825)
XLA Ops:
  7.2 1.2 slice.18
  8.4 0.7 slice_bitcast_fusion
  9.1 0.6 compare_convert_fusion
  9.8 1.1 copy.20
  10.8 0.7 concatenate.24
  12.0 1.2 copy.19
  14.4 0.7 copy.24
  15.4 6.7 %convolution_convert_fusion = bf16[2560,2560]{1,0:T(8,128)(2,1)} fusion(bf16[256,2560]{0,1:T(8,128)(2,1)S(1)} %bitcast.111, bf16[128,2560]{1,0:T(8,128)(2,1)S(1)} %copy-done.4, bf16[128,2560]{1,0:T(8,128)(2,1)S(1)} %copy-done), kind=kOutput, calls=%fused_computation.1 | convolution fusion | flops 3364618240 | bytes 15728640 | tf_op jit(solution)/shard_map/dot_general | solution.py:84
  22.2 107.0 %reduce-scatter.2.cloned.1.call-done = bf16[80,2560]{1,0:T(8,128)(2,1)} async-done(((bf16[2560,2560]{1,0:T(8,128)(2,1)}), bf16[80,2560]{1,0:T(8,128)(2,1)}) %reduce-scatter.2.cloned.1.call-update) | async-done | bytes 409616 | tf_op jit(solution)/shard_map/reduce_scatter | solution.py:85
  129.2 1.1 bitcast_add_fusion
  135.5 0.7 multiply_convert_fusion
  136.7 0.8 multiply_reduce_fusion.1
  138.2 0.7 fusion.27
  139.0 0.7 convolution_add_fusion.8
  139.8 0.7 fusion.38
  140.6 0.7 convolution_add_fusion.7
  141.3 0.7 fusion.39
  142.1 0.7 convolution_add_fusion.6
  142.9 0.7 fusion.40
  143.7 0.7 convolution_add_fusion.5
  144.4 0.7 fusion.41
  145.2 1.4 fusion.3
  146.7 10.7 %all-gather.2 = bf16[512,256]{1,0:T(8,128)(2,1)S(1)} all-gather(bf16[128,256]{1,0:T(8,128)(2,1)S(1)} %copy-done.5), channel_id=4, replica_groups=mesh['dp'=32,'tensor'=4] {'tensor'}, dimensions={0}, use_global_device_ids=true | all-gather | bytes 327680 | tf_op jit(solution)/shard_map/all_gather | solution.py:54
  157.4 1.2 fusion.46
  158.7 4.7 collective-permute-start
  163.3 5.0 %collective-permute-done = f32[256,2560]{1,0:T(8,128)S(1)} collective-permute-done((f32[256,2560]{1,0:T(8,128)S(1)}, f32[256,2560]{1,0:T(8,128)S(1)}, u32[]{:S(2)}, u32[]{:S(2)}) %collective-permute-start) | collective-permute-done | bytes 2621472 | tf_op jit(solution)/shard_map/ppermute | solution.py:65
  169.1 81.1 %collective-permute-done.1 = f32[256,2560]{1,0:T(8,128)S(1)} collective-permute-done((f32[256,2560]{1,0:T(8,128)S(1)}, f32[256,2560]{1,0:T(8,128)S(1)}, u32[]{:S(2)}, u32[]{:S(2)}) %collective-permute-start.1) | collective-permute-done | bytes 2621472 | tf_op jit(solution)/shard_map/ppermute | solution.py:65
  250.5 1.9 collective-permute-start.2
  252.4 61.6 %collective-permute-done.2 = f32[256,2560]{1,0:T(8,128)S(1)} collective-permute-done((f32[256,2560]{1,0:T(8,128)S(1)}, f32[256,2560]{1,0:T(8,128)S(1)}, u32[]{:S(2)}, u32[]{:S(2)}) %collective-permute-start.2) | collective-permute-done | bytes 2621472 | tf_op jit(solution)/shard_map/ppermute | solution.py:65
  314.3 1.2 collective-permute-start.3
  315.6 55.8 %collective-permute-done.3 = f32[256,2560]{1,0:T(8,128)S(1)} collective-permute-done((f32[256,2560]{1,0:T(8,128)S(1)}, f32[256,2560]{1,0:T(8,128)S(1)}, u32[]{:S(2)}, u32[]{:S(2)}) %collective-permute-start.3) | collective-permute-done | bytes 2621472 | tf_op jit(solution)/shard_map/ppermute | solution.py:65
  371.7 3.6 collective-permute-start.4
  377.3 53.2 %collective-permute-done.4 = f32[256,2560]{1,0:T(8,128)} collective-permute-done((f32[256,2560]{1,0:T(8,128)S(1)}, f32[256,2560]{1,0:T(8,128)}, u32[]{:S(2)}, u32[]{:S(2)}) %collective-permute-start.4) | collective-permute-done | bytes 2621472 | tf_op jit(solution)/shard_map/ppermute | solution.py:65
  430.4 2.0 add.188
  432.5 0.7 multiply_reduce_fusion
  433.2 2.8 fusion.37
  436.3 2.4 fusion.36
  438.7 3.2 fusion.26
  442.2 3.2 convolution_add_fusion.3
  445.4 2.5 fusion.47
  448.2 2.6 convolution_add_fusion.2
  450.7 2.5 fusion.48
  453.5 2.6 convolution_add_fusion.1
  456.2 2.8 fusion.49
  459.2 3.7 fusion.1
  463.0 1.6 copy.25
  464.6 1.5 dynamic-slice_bitcast_fusion
  466.1 9.9 %gather_fusion = bf16[30,64,2560]{2,1,0:T(8,128)(2,1)} fusion(bf16[32,64,2560]{2,1,0:T(8,128)(2,1)} %bitcast.109, s32[1024]{0:T(1024)S(1)} %pad_clamp_fusion), kind=kCustom, calls=%fused_computation | custom fusion | bytes 19660920 | tf_op jit(solution)/shard_map/jit(_take)/gather | solution.py:96
  (63 shorter events, 11.0 us)
Async XLA Ops:
  7.2 122.0 %reduce-scatter.2.cloned.1.call-start = ((), (), s32[]{:S(2)}) async-start(), calls=%async_computation.1 | async-start | bytes 13516800 | tf_op jit(solution)/shard_map/reduce_scatter | solution.py:85
  14.1 1.1 copy-start
  14.1 1.3 copy-start.4
  22.1 107.1 %copy-start.3 = (f32[1,74,2560]{2,0,1:T(1,128)S(1)}, f32[1,74,2560]{2,0,1:T(1,128)}, u32[]{:S(2)}) copy-start(f32[1,74,2560]{2,0,1:T(1,128)} %param.16) | copy-start | bytes 2273284
  22.2 442.5 %all-gather.8.cloned.1.call-start = ((), (), s32[]{:S(2)}) async-start(), calls=%async_computation.3 | async-start | bytes 2703360 | tf_op jit(solution)/shard_map/all_gather | solution.py:93
  136.2 330.0 %all-gather.6.cloned.1.call-start = ((), (), s32[]{:S(2)}) async-start(), calls=%async_computation.2 | async-start | bytes 10813440 | tf_op jit(solution)/shard_map/all_gather | solution.py:89
  142.8 3.8 copy-start.5
  158.7 9.7 %collective-permute-start = (f32[256,2560]{1,0:T(8,128)S(1)}, f32[256,2560]{1,0:T(8,128)S(1)}, u32[]{:S(2)}, u32[]{:S(2)}) collective-permute-start(f32[256,2560]{1,0:T(8,128)S(1)} %fusion.46), channel_id=1, source_target_pairs={{0,4},{4,0},{8,12},{12,8},{16,20},{20,16},{24,28},{28,24},{32,36},... | collective-permute-start | bytes 7864328 | tf_op jit(solution)/shard_map/ppermute | solution.py:65
  168.6 81.6 %collective-permute-start.1 = (f32[256,2560]{1,0:T(8,128)S(1)}, f32[256,2560]{1,0:T(8,128)S(1)}, u32[]{:S(2)}, u32[]{:S(2)}) collective-permute-start(f32[256,2560]{1,0:T(8,128)S(1)} %add.184), channel_id=1, source_target_pairs={{0,8},{4,12},{8,0},{12,4},{16,24},{20,28},{24,16},{28,20},{32,40},... | collective-permute-start | bytes 7864328 | tf_op jit(solution)/shard_map/ppermute | solution.py:65
  250.5 63.5 %collective-permute-start.2 = (f32[256,2560]{1,0:T(8,128)S(1)}, f32[256,2560]{1,0:T(8,128)S(1)}, u32[]{:S(2)}, u32[]{:S(2)}) collective-permute-start(f32[256,2560]{1,0:T(8,128)S(1)} %add.185), channel_id=1, source_target_pairs={{0,16},{4,20},{8,24},{12,28},{16,0},{20,4},{24,8},{28,12},{32,48},... | collective-permute-start | bytes 7864328 | tf_op jit(solution)/shard_map/ppermute | solution.py:65
  314.3 57.1 %collective-permute-start.3 = (f32[256,2560]{1,0:T(8,128)S(1)}, f32[256,2560]{1,0:T(8,128)S(1)}, u32[]{:S(2)}, u32[]{:S(2)}) collective-permute-start(f32[256,2560]{1,0:T(8,128)S(1)} %add.186), channel_id=1, source_target_pairs={{0,32},{4,36},{8,40},{12,44},{16,48},{20,52},{24,56},{28,60},{32,0... | collective-permute-start | bytes 7864328 | tf_op jit(solution)/shard_map/ppermute | solution.py:65
  371.7 58.7 %collective-permute-start.4 = (f32[256,2560]{1,0:T(8,128)S(1)}, f32[256,2560]{1,0:T(8,128)}, u32[]{:S(2)}, u32[]{:S(2)}) collective-permute-start(f32[256,2560]{1,0:T(8,128)S(1)} %add.187), channel_id=1, source_target_pairs={{0,64},{4,68},{8,72},{12,76},{16,80},{20,84},{24,88},{28,92},{32,9... | collective-permute-start | bytes 7864328 | tf_op jit(solution)/shard_map/ppermute | solution.py:65
  377.3 55.2 %copy-start.1 = (f32[2,128,2560]{2,1,0:T(8,128)S(1)}, f32[2,128,2560]{2,1,0:T(8,128)}, u32[]{:S(2)}) copy-start(f32[2,128,2560]{2,1,0:T(8,128)} %param.17) | copy-start | bytes 7864324
  433.2 8.9 %copy-start.2 = (f32[2,128,2560]{2,1,0:T(8,128)}, f32[2,128,2560]{2,1,0:T(8,128)S(1)}, u32[]{:S(2)}) copy-start(f32[2,128,2560]{2,1,0:T(8,128)S(1)} %get-tuple-element.16) | copy-start | bytes 7864324
Sparse Core Ops, SparseCore 0:
  22.3 106.8 reduce-scatter.1
  136.3 47.6 all-gather.7
  186.8 74.6 all-gather.5
